TPU v7x, 512 devices: a whole 4x4x16 slice. The times are simulated.
512 devices in a mesh: section: 32 (over z_lo, y, core), seq: 16 (over x, z_hi).
Axes of the slice: x: 4, y: 4, z: 16 (z_hi: 4, z_lo: 4; z = z_hi * 4 + z_lo), core: 2. Of those that a mesh axis runs over, the one named last changes fastest.
Arguments:
- up_activation: bfloat16 [32, 2048, 4096], P('section', 'seq'), as said below
- saved_projections: bfloat16 [32, 2048, 768], P('section', 'seq'), as said below
- up_cotangent: bfloat16 [32, 2048, 4096], P('section', 'seq'), may hold values from -6 to 6
- up_input_weight: bfloat16 [32, 4096, 768], P('section', 'seq'), may hold values from -0.09375 to 0.09375
- up_output_weight: bfloat16 [32, 512, 4096], P('section', None, 'seq'), may hold values from -0.25 to 0.25
- upward_gain: float32 [32, 4096], P('section'), may hold values from 0.5 to 1.5
- accum_input: bfloat16 [32, 4096, 768], P('section', 'seq'), may hold values from -48 to 48
- doc_starts: int32 [32, 2048], P('section', 'seq'), may hold values from 0 to 2047, as said below
Outputs:
- upward_grad: bfloat16 [32, 2048, 4096], P('section', 'seq')
- project_grads: bfloat16 [32, 4096, 768], P('section', 'seq')
Inputs may be any that keep to these rules, and one draw needn't show every extreme that they name: doc_starts[s, t] is the position of the first token of the document holding token t: it is 0 at t = 0, equals t or doc_starts[s, t - 1] elsewhere, and the last token of every micro-batch starts a document. `up_activation`: saved inputs of the upward layers. `saved_projections`: saved queries, keys and values of the upward layers.
All inputs are finite; a program needn't handle non-finite values.
Results may differ from a plain program's by a relative error of at most 0.014.
Values may be sent and summed in bfloat16 or wider, within the bound.
No kernel may reach another device: no remote copies, remote signals or barrier semaphores. Data moves between devices by JAX's collectives and lax.ppermute only.
A program may use at most 64 MiB of HBM per device.

v0:
```python
import jax
import jax.numpy as jnp
from jax import lax
from jax.sharding import PartitionSpec as P

HEAD = 128
GROUP = 4


def shifted(value, axis, steps):
    count = lax.axis_size(axis)
    initial, last = (max(0, -steps), min(count, count - steps))
    return lax.ppermute(value, axis, [(source, source + steps) for source in range(initial, last)])


def from_partner(x, axis, stride):
    return lax.ppermute(x, axis, [(i, i ^ 1 << stride) for i in range(lax.axis_size(axis))])


def contract_last(left, right):
    return lax.dot_general(
        left, right, (((1,), (1,)), ((), ())), preferred_element_type=jnp.float32
    )


def contract_first(left, right):
    return lax.dot_general(
        left, right, (((0,), (0,)), ((), ())), preferred_element_type=jnp.float32
    )


def normalize(values, gain):
    floats = values.astype(jnp.float32)
    inverse = lax.rsqrt(jnp.mean(floats * floats, axis=-1, keepdims=True) + 1e-05)
    unit = floats * inverse
    return (unit, inverse, unit * gain)


def per_device(
    up_activation,
    saved_projections,
    up_cotangent,
    up_input_weight,
    up_output_weight,
    upward_gain,
    accum_input,
    doc_starts,
):
    factor = HEAD ** (-0.5)
    width = GROUP * HEAD
    count = up_activation.shape[1]
    first = lax.axis_index("seq") * count
    saved = saved_projections[0]
    cotangent = up_cotangent[0]
    unit_up, inverse_up, normed_up = normalize(up_activation[0], upward_gain[0])
    hidden = normed_up.astype(jnp.bfloat16)
    key_value = lax.all_gather(saved[:, width:], "seq", axis=0, tiled=True)
    keys = key_value[:, :HEAD]
    values = key_value[:, HEAD:]
    query = saved[:, :width].reshape(count, GROUP, HEAD)
    hidden_cols = lax.all_to_all(hidden, "seq", split_axis=1, concat_axis=0, tiled=True)
    block = cotangent
    attn_grad = contract_last(
        block, lax.all_gather(up_output_weight[0], "seq", axis=1, tiled=True)
    ).astype(jnp.bfloat16)
    positions = first + jnp.arange(count, dtype=jnp.int32)
    key_positions = jnp.arange(keys.shape[0], dtype=jnp.int32)
    starts = doc_starts[0]
    visible = (key_positions[None, :] <= positions[:, None]) & (
        key_positions[None, :] >= starts[:, None]
    )
    scores = jnp.einsum("tgh,jh->tgj", query, keys, preferred_element_type=jnp.float32) * factor
    scores = jnp.where(visible[:, None, :], scores, -1e30)
    top = jnp.max(scores, axis=-1, keepdims=True)
    exps = jnp.where(visible[:, None, :], jnp.exp(scores - top), 0.0)
    probs = exps / jnp.sum(exps, axis=-1, keepdims=True)
    weights = probs.astype(jnp.bfloat16)
    grad_heads = attn_grad.reshape(count, GROUP, HEAD)
    prob_grad = jnp.einsum("tgh,jh->tgj", grad_heads, values, preferred_element_type=jnp.float32)
    inner = jnp.sum(probs * prob_grad, axis=-1, keepdims=True)
    score_grad = (probs * (prob_grad - inner) * factor).astype(jnp.bfloat16)
    query_grad = (
        jnp.einsum("tgj,jh->tgh", score_grad, keys, preferred_element_type=jnp.float32)
        .astype(jnp.bfloat16)
        .reshape(count, width)
    )
    key_part = jnp.einsum("tgj,tgh->jh", score_grad, query, preferred_element_type=jnp.float32)
    value_part = jnp.einsum("tgj,tgh->jh", weights, grad_heads, preferred_element_type=jnp.float32)
    key_total, value_total = (
        lax.psum(key_part.astype(jnp.bfloat16), "seq").astype(jnp.float32),
        lax.psum(value_part.astype(jnp.bfloat16), "seq").astype(jnp.float32),
    )
    kv_grad = jnp.concatenate(
        [key_total.astype(jnp.bfloat16), value_total.astype(jnp.bfloat16)], axis=1
    )
    query_all = lax.all_gather(query_grad, "seq", axis=0, tiled=True)
    grad_all = jnp.concatenate([query_all, kv_grad], axis=1)
    input_term = contract_first(hidden_cols, grad_all).astype(jnp.bfloat16)
    block = contract_last(grad_all, up_input_weight[0])
    hidden_grad = lax.all_to_all(block, "seq", split_axis=0, concat_axis=1, tiled=True)
    scaled = hidden_grad * upward_gain[0]
    input_grad = cotangent.astype(jnp.float32) + inverse_up * (
        scaled - unit_up * jnp.mean(scaled * unit_up, axis=-1, keepdims=True)
    )
    moved_grad = shifted(input_grad.astype(jnp.bfloat16), "section", 1)
    sections = lax.axis_size("section")
    mirror_input = input_term
    for bit in range(sections.bit_length() - 1):
        mirror_input = from_partner(mirror_input, "section", bit)
    project_grads = (accum_input[0].astype(jnp.float32) + mirror_input.astype(jnp.float32)).astype(
        jnp.bfloat16
    )
    return (moved_grad[None], project_grads[None])


def solution(mesh):
    return jax.shard_map(
        per_device,
        mesh=mesh,
        in_specs=(
            P("section", "seq", None),
            P("section", "seq", None),
            P("section", "seq", None),
            P("section", "seq", None),
            P("section", None, "seq"),
            P("section", None),
            P("section", "seq", None),
            P("section", "seq"),
        ),
        out_specs=(P("section", "seq", None), P("section", "seq", None)),
        check_vma=False,
    )
```

profile of v0, /device:TPU:25, one launch (start us, length us, event | category | flops | bytes accessed | tf_op | source)
XLA Modules:
  0.0 827.4 jit_solution(4818707884297721254)
XLA Ops:
  7.2 1.5 slice.17
  8.8 0.7 all-gather.9.cloned.1.call-update
  9.6 1.1 fusion.37
  10.7 82.6 %all-gather.5.cloned.1.call-done = bf16[2048,256]{1,0:T(8,128)(2,1)} async-done(((bf16[128,256]{1,0:T(8,128)(2,1)}), bf16[2048,256]{1,0:T(8,128)(2,1)}) %all-gather.5.cloned.1.call-update) | async-done | bytes 1048592 | tf_op jit(solution)/shard_map/all_gather | solution.py:57
  93.3 5.0 fusion.64
  98.4 136.5 %all-gather.9.cloned.1.call-done = bf16[1,512,4096]{2,1,0:T(8,128)(2,1)} async-done(((bf16[1,512,256]{2,1,0:T(8,128)(2,1)}), bf16[1,512,4096]{2,1,0:T(8,128)(2,1)}) %all-gather.9.cloned.1.call-update) | async-done | bytes 4194320 | tf_op jit(solution)/shard_map/all_gather | solution.py:64
  234.9 3.9 fusion.33
  238.8 1.8 fusion.9
  240.5 2.7 fusion.41
  243.2 8.2 fusion.8
  251.4 0.0 all-gather.7.cloned.1.call-start
  251.5 9.2 %fusion.27 = bf16[128,4,128]{0,2,1:T(8,128)(2,1)} fusion(f32[128,4,2048]{2,0,1:T(8,128)} %fusion.41, bf16[2048,256]{1,0:T(8,128)(2,1)S(1)} %copy-done.6, f32[128,4,2048]{2,0,1:T(8,128)} %get-tuple-element.9, f32[128,4]{0,1:T(4,128)S(1)} %get-tuple-element.8), kind=kOutput, calls=%fused_computation.35 | convolution fusion | flops 275843584 | bytes 17436672 | tf_op jit(solution)/shard_map/tgj,jh->tgh/dot_general | solution.py:83
  260.7 195.4 %all-reduce.3.cloned.1.call-done = (bf16[2048,128]{1,0:T(8,128)(2,1)}, bf16[2048,128]{1,0:T(8,128)(2,1)}) async-done(((bf16[2048,128]{1,0:T(8,128)(2,1)}, bf16[2048,128]{1,0:T(8,128)(2,1)}), (bf16[2048,128]{1,0:T(8,128)(2,1)}, bf16[2048,128]{1,0:T(8,128)(2,1)})) %all-reduce.3.cloned.1.call-update) | async-done | bytes 1048592 | tf_op jit(solution)/shard_map/psum | solution.py:91
  456.1 2.0 copy.29
  458.2 2.0 copy.30
  460.2 102.7 %all-gather.7.cloned.1.call-done = bf16[2048,512]{0,1:T(8,128)(2,1)} async-done(((bf16[128,512]{0,1:T(8,128)(2,1)}), bf16[2048,512]{0,1:T(8,128)(2,1)}) %all-gather.7.cloned.1.call-update) | async-done | bytes 2097168 | tf_op jit(solution)/shard_map/all_gather | solution.py:96
  562.9 2.0 pad_maximum_fusion
  565.0 2.8 copy.31
  567.8 4.2 fusion.43
  572.1 10.1 %all-to-all-start = ((f32[16,128,256]{2,1,0:T(8,128)}), f32[16,128,256]{2,1,0:T(8,128)S(1)}, u32[]{:S(2)}, u32[]{:S(2)}) async-start(f32[16,128,256]{2,1,0:T(8,128)} %fusion.43), calls=%async_computation | async-start | bytes 4194304 | tf_op jit(solution)/shard_map/all_to_all | solution.py:100
  582.2 1.6 copy.21
  583.8 1.6 copy.33
  585.5 0.6 broadcast.82
  586.0 1.3 reduce.4
  587.4 1.3 mul.85
  588.7 0.6 fusion.19
  589.2 0.5 add_rsqrt_fusion
  589.8 73.2 %all-to-all-done = f32[16,128,256]{2,1,0:T(8,128)S(1)} async-done(((f32[16,128,256]{2,1,0:T(8,128)}), f32[16,128,256]{2,1,0:T(8,128)S(1)}, u32[]{:S(2)}, u32[]{:S(2)}) %all-to-all-start) | async-done | bytes 2097184 | tf_op jit(solution)/shard_map/all_to_all | solution.py:100
  662.9 3.1 multiply_convert_fusion.1
  666.0 76.9 %all_to_all.32 = bf16[128,16,256]{2,0,1:T(8,128)(2,1)S(1)} all-to-all(bf16[128,16,256]{2,0,1:T(8,128)(2,1)S(1)} %get-tuple-element.6), channel_id=1, replica_groups=mesh['section'=32,'seq'=16] {'seq'}, dimensions={1} | all-to-all | bytes 2097152 | tf_op jit(solution)/shard_map/all_to_all | solution.py:61
  742.9 1.0 convolution_convert_fusion
  743.9 5.6 collective-permute-start.1
  749.5 1.5 collective-permute-done.1
  751.0 1.9 collective-permute-start.2
  752.9 2.3 copy.20
  755.2 1.8 copy.32
  757.0 0.7 broadcast_multiply_fusion
  757.8 5.8 collective-permute-done.2
  763.5 1.9 collective-permute-start.3
  765.4 2.3 fusion.18
  767.7 1.9 collective-permute-start
  769.7 6.8 collective-permute-done.3
  776.5 8.9 %collective-permute-start.4 = (bf16[256,768]{1,0:T(8,128)(2,1)S(1)}, bf16[256,768]{1,0:T(8,128)(2,1)S(1)}, u32[]{:S(2)}, u32[]{:S(2)}) collective-permute-start(bf16[256,768]{1,0:T(8,128)(2,1)S(1)} %collective-permute-done.3), channel_id=1, source_target_pairs={{0,128},{16,144},{32,160},{48,176},{64,192},{80,208},{96,224},{112... | collective-permute-start | bytes 1179656 | tf_op jit(solution)/shard_map/ppermute | solution.py:17
  785.4 6.4 collective-permute-done.4
  791.8 11.7 %collective-permute-start.5 = (bf16[256,768]{1,0:T(8,128)(2,1)S(1)}, bf16[256,768]{1,0:T(8,128)(2,1)S(1)}, u32[]{:S(2)}, u32[]{:S(2)}) collective-permute-start(bf16[256,768]{1,0:T(8,128)(2,1)S(1)} %collective-permute-done.4), channel_id=1, source_target_pairs={{0,256},{16,272},{32,288},{48,304},{64,320},{80,336},{96,352},{112... | collective-permute-start | bytes 1179656 | tf_op jit(solution)/shard_map/ppermute | solution.py:17
  803.5 1.3 copy.34
  804.8 15.2 %collective-permute-done.5 = bf16[256,768]{1,0:T(8,128)(2,1)S(1)} collective-permute-done((bf16[256,768]{1,0:T(8,128)(2,1)S(1)}, bf16[256,768]{1,0:T(8,128)(2,1)S(1)}, u32[]{:S(2)}, u32[]{:S(2)}) %collective-permute-start.5) | collective-permute-done | bytes 393248 | tf_op jit(solution)/shard_map/ppermute | solution.py:17
  820.1 0.8 fusion.42
  (28 shorter events, 0.2 us)
Async XLA Ops:
  7.2 560.7 %copy-start = (bf16[1,256,768]{2,1,0:T(8,128)(2,1)S(1)}, bf16[1,256,768]{2,1,0:T(8,128)(2,1)}, u32[]{:S(2)}) copy-start(bf16[1,256,768]{2,1,0:T(8,128)(2,1)} %param.11) | copy-start | bytes 1179652
  7.2 86.2 %all-gather.5.cloned.1.call-start = ((), (), s32[]{:S(2)}) async-start(), calls=%async_computation.2 | async-start | bytes 1114112 | tf_op jit(solution)/shard_map/all_gather | solution.py:57
  8.8 226.1 %all-gather.9.cloned.1.call-start = ((), (), s32[]{:S(2)}) async-start(), calls=%async_computation.4 | async-start | bytes 4456448 | tf_op jit(solution)/shard_map/all_gather | solution.py:64
  9.5 446.6 %all-reduce.3.cloned.1.call-start = ((), (), s32[]{:S(2)}) async-start(), calls=%async_computation.5 | async-start | bytes 2097152 | tf_op jit(solution)/shard_map/psum | solution.py:91
  10.7 224.2 %copy-start.1 = (bf16[1,128,4096]{2,1,0:T(8,128)(2,1)S(1)}, bf16[1,128,4096]{2,1,0:T(8,128)(2,1)}, u32[]{:S(2)}) copy-start(bf16[1,128,4096]{2,1,0:T(8,128)(2,1)} %param.10) | copy-start | bytes 3145732
  234.9 3.9 copy-start.9
  238.8 1.8 copy-start.6
  240.5 2.7 copy-start.8
  251.4 311.5 %all-gather.7.cloned.1.call-start = ((), (), s32[]{:S(2)}) async-start(), calls=%async_computation.3 | async-start | bytes 2228224 | tf_op jit(solution)/shard_map/all_gather | solution.py:96
  572.1 14.0 %copy-start.7 = (f32[1,4096]{1,0:T(1,128)S(1)}, f32[1,4096]{1,0:T(1,128)}, u32[]{:S(2)}) copy-start(f32[1,4096]{1,0:T(1,128)} %param.13) | copy-start | bytes 49156
  572.1 90.9 %all-to-all-start = ((f32[16,128,256]{2,1,0:T(8,128)}), f32[16,128,256]{2,1,0:T(8,128)S(1)}, u32[]{:S(2)}, u32[]{:S(2)}) async-start(f32[16,128,256]{2,1,0:T(8,128)} %fusion.43), calls=%async_computation | async-start | bytes 4194304 | tf_op jit(solution)/shard_map/all_to_all | solution.py:100
  662.9 80.0 %copy-start.2 = (bf16[2048,512]{0,1:T(8,128)(2,1)S(1)}, bf16[2048,512]{0,1:T(8,128)(2,1)}, u32[]{:S(2)}) copy-start(bf16[2048,512]{0,1:T(8,128)(2,1)} %all-gather.7.cloned.1.call-done) | copy-start | bytes 6291460
  662.9 80.0 %copy-start.3 = (bf16[2048,128]{0,1:T(8,128)(2,1)S(1)}, bf16[2048,128]{0,1:T(8,128)(2,1)}, u32[]{:S(2)}) copy-start(bf16[2048,128]{0,1:T(8,128)(2,1)} %copy.29) | copy-start | bytes 1572868
  662.9 80.0 %copy-start.4 = (bf16[2048,128]{0,1:T(8,128)(2,1)S(1)}, bf16[2048,128]{0,1:T(8,128)(2,1)}, u32[]{:S(2)}) copy-start(bf16[2048,128]{0,1:T(8,128)(2,1)} %copy.30) | copy-start | bytes 1572868
  743.9 7.1 collective-permute-start.1
  751.0 12.5 %collective-permute-start.2 = (bf16[256,768]{1,0:T(8,128)(2,1)}, bf16[256,768]{1,0:T(8,128)(2,1)}, u32[]{:S(2)}, u32[]{:S(2)}) collective-permute-start(bf16[256,768]{1,0:T(8,128)(2,1)} %collective-permute-done.1), channel_id=1, source_target_pairs={{0,32},{16,48},{32,0},{48,16},{64,96},{80,112},{96,64},{112,80},{1... | collective-permute-start | bytes 1179656 | tf_op jit(solution)/shard_map/ppermute | solution.py:17
  757.0 63.1 %copy-start.5 = (bf16[1,256,768]{2,1,0:T(8,128)(2,1)S(1)}, bf16[1,256,768]{2,1,0:T(8,128)(2,1)}, u32[]{:S(2)}) copy-start(bf16[1,256,768]{2,1,0:T(8,128)(2,1)} %param.14) | copy-start | bytes 1179652
  763.5 13.0 %collective-permute-start.3 = (bf16[256,768]{1,0:T(8,128)(2,1)}, bf16[256,768]{1,0:T(8,128)(2,1)S(1)}, u32[]{:S(2)}, u32[]{:S(2)}) collective-permute-start(bf16[256,768]{1,0:T(8,128)(2,1)} %collective-permute-done.2), channel_id=1, source_target_pairs={{0,64},{16,80},{32,96},{48,112},{64,0},{80,16},{96,32},{112,48},{1... | collective-permute-start | bytes 1179656 | tf_op jit(solution)/shard_map/ppermute | solution.py:17
  767.7 35.8 %collective-permute-start = (bf16[128,4096]{0,1:T(8,128)(2,1)S(1)}, bf16[128,4096]{0,1:T(8,128)(2,1)S(1)}, u32[]{:S(2)}, u32[]{:S(2)}) collective-permute-start(bf16[128,4096]{0,1:T(8,128)(2,1)S(1)} %fusion.18), channel_id=1, source_target_pairs={{0,16},{16,32},{32,48},{48,64},{64,80},{80,96},{96,112},{112,128},... | collective-permute-start | bytes 3145736 | tf_op jit(solution)/shard_map/ppermute | solution.py:13
  776.5 15.3 %collective-permute-start.4 = (bf16[256,768]{1,0:T(8,128)(2,1)S(1)}, bf16[256,768]{1,0:T(8,128)(2,1)S(1)}, u32[]{:S(2)}, u32[]{:S(2)}) collective-permute-start(bf16[256,768]{1,0:T(8,128)(2,1)S(1)} %collective-permute-done.3), channel_id=1, source_target_pairs={{0,128},{16,144},{32,160},{48,176},{64,192},{80,208},{96,224},{112... | collective-permute-start | bytes 1179656 | tf_op jit(solution)/shard_map/ppermute | solution.py:17
  791.8 28.2 %collective-permute-start.5 = (bf16[256,768]{1,0:T(8,128)(2,1)S(1)}, bf16[256,768]{1,0:T(8,128)(2,1)S(1)}, u32[]{:S(2)}, u32[]{:S(2)}) collective-permute-start(bf16[256,768]{1,0:T(8,128)(2,1)S(1)} %collective-permute-done.4), channel_id=1, source_target_pairs={{0,256},{16,272},{32,288},{48,304},{64,320},{80,336},{96,352},{112... | collective-permute-start | bytes 1179656 | tf_op jit(solution)/shard_map/ppermute | solution.py:17
Sparse Core Ops, SparseCore 0:
  11.6 81.7 all-gather.4
  96.3 138.4 all-gather.8
  251.5 204.5 all-reduce.2
  460.0 102.9 all-gather.6
where the time goes:
time: 828 us; the launch traced here: 827 us
  waiting for transfers between devices  627 us (76%)
  blocking collectives  76.9 us (9%)
  starting transfers between devices  42.2 us (5%)
  matrix products  36 us (4%)
  local copies, waits for them, and re-layouts  19.1 us (2%)
  between operations  13.9 us (2%)
  other arithmetic  12.5 us (2%)
    psum x1, waiting for transfers between devices, per_device(): lax.psum(value_part.astype(jnp.bfloat16), 'seq').astype(jnp.float32)  195 us
    all_gather x1, waiting for transfers between devices, per_device(): lax.all_gather(up_output_weight[0], 'seq', axis=1, tiled=True)  137 us
    all_gather x1, waiting for transfers between devices, per_device(): query_all = lax.all_gather(query_grad, 'seq', axis=0, tiled=True)  103 us
    all_gather x1, waiting for transfers between devices, per_device(): key_value = lax.all_gather(saved[:, width:], 'seq', axis=0, tiled=True)  82.6 us
    all_to_all x1, blocking collectives, per_device(): lax.all_to_all(hidden, 'seq', split_axis=1, concat_axis=0, tiled=True)  76.9 us
    all_to_all x1, waiting for transfers between devices, per_device(): lax.all_to_all(block, 'seq', split_axis=0, concat_axis=1, tiled=True)  73.2 us
    ppermute x5, waiting for transfers between devices, from_partner(): lax.ppermute(x, axis, [(i, i ^ 1 << stride) for i in range(lax.axis_size(...  35.7 us
    ppermute x5, starting transfers between devices, from_partner(): lax.ppermute(x, axis, [(i, i ^ 1 << stride) for i in range(lax.axis_size(...  30 us
  transfers between devices with their start and end apart: 11, of which 10 were waited for; matrix products, arithmetic and copies ran while one was open for 4% of the time, Pallas kernels for 0%

commit v1 on v0

--- a/solution.py
+++ b/solution.py
@@ -54,7 +54,9 @@
     cotangent = up_cotangent[0]
     unit_up, inverse_up, normed_up = normalize(up_activation[0], upward_gain[0])
     hidden = normed_up.astype(jnp.bfloat16)
-    key_value = lax.all_gather(saved[:, width:], "seq", axis=0, tiled=True)
+    key_value = jnp.concatenate(
+        lax.all_to_all(jnp.stack([saved[:, width:]] * lax.axis_size("seq")), "seq", 0, 0), axis=0
+    )
     keys = key_value[:, :HEAD]
     values = key_value[:, HEAD:]
     query = saved[:, :width].reshape(count, GROUP, HEAD)

time: 828 us -> 782 us (0.944)
  waiting for transfers between devices: 627 us -> 566 us
  starting transfers between devices: 42.2 us -> 61.6 us
    all_gather x1 -> x0, waiting for transfers between devices: 82.6 us -> none  [per_device(): key_value = lax.all_gather(saved[:, width:], 'seq', axis=0, tiled=True)]
    all_to_all x0 -> x1, waiting for transfers between devices: none -> 60.4 us  [per_device(): lax.all_to_all(jnp.stack([saved[:, width:]] * lax.axis_size('seq')), 'seq...]
    all_gather x1, waiting for transfers between devices: 137 us -> 97.4 us  [per_device(): lax.all_gather(up_output_weight[0], 'seq', axis=1, tiled=True)]
    all_to_all x0 -> x1, starting transfers between devices: none -> 17.4 us  [per_device(): lax.all_to_all(jnp.stack([saved[:, width:]] * lax.axis_size('seq')), 'seq...]
  transfers between devices with their start and end apart: 11 -> 11, of which waited for: 10 -> 10; matrix products, arithmetic and copies ran while one was open for 4% -> 5% of each run, Pallas kernels for 0% -> 0%
where the time goes in v1:
time: 782 us; the launch traced here: 781 us
  waiting for transfers between devices  566 us (72%)
  blocking collectives  71.6 us (9%)
  starting transfers between devices  61.6 us (8%)
  matrix products  37 us (5%)
  local copies, waits for them, and re-layouts  19.8 us (3%)
  between operations  13.9 us (2%)
  other arithmetic  11.7 us (1%)
    psum x1, waiting for transfers between devices, per_device(): lax.psum(value_part.astype(jnp.bfloat16), 'seq').astype(jnp.float32)  196 us
    all_gather x1, waiting for transfers between devices, per_device(): query_all = lax.all_gather(query_grad, 'seq', axis=0, tiled=True)  103 us
    all_gather x1, waiting for transfers between devices, per_device(): lax.all_gather(up_output_weight[0], 'seq', axis=1, tiled=True)  97.4 us
    all_to_all x1, waiting for transfers between devices, per_device(): lax.all_to_all(block, 'seq', split_axis=0, concat_axis=1, tiled=True)  73.2 us
    all_to_all x1, blocking collectives, per_device(): lax.all_to_all(hidden, 'seq', split_axis=1, concat_axis=0, tiled=True)  71.6 us
    all_to_all x1, waiting for transfers between devices, per_device(): lax.all_to_all(jnp.stack([saved[:, width:]] * lax.axis_size('seq')), 'seq...  60.4 us
    ppermute x5, waiting for transfers between devices, from_partner(): lax.ppermute(x, axis, [(i, i ^ 1 << stride) for i in range(lax.axis_size(...  35.4 us
    ppermute x5, starting transfers between devices, from_partner(): lax.ppermute(x, axis, [(i, i ^ 1 << stride) for i in range(lax.axis_size(...  30.7 us
  transfers between devices with their start and end apart: 11, of which 10 were waited for; matrix products, arithmetic and copies ran while one was open for 5% of the time, Pallas kernels for 0%

profile of v1, /device:TPU:25, one launch (start us, length us, event | category | flops | bytes accessed | tf_op | source)
XLA Modules:
  0.0 781.2 jit_solution(9324347004490086419)
XLA Ops:
  7.2 0.7 all-gather.6.cloned.1.call-update
  7.9 1.1 copy.20
  9.1 1.1 stack.2
  10.2 17.4 %all-to-all-start = ((bf16[16,128,256]{2,1,0:T(8,128)(2,1)}), bf16[16,128,256]{2,1,0:T(8,128)(2,1)S(1)}, u32[]{:S(2)}, u32[]{:S(2)}) async-start(bf16[16,128,256]{2,1,0:T(8,128)(2,1)} %stack.2), calls=%async_computation | async-start | bytes 2097152 | tf_op jit(solution)/shard_map/all_to_all | solution.py:58
  28.2 60.4 %all-to-all-done = bf16[16,128,256]{2,1,0:T(8,128)(2,1)S(1)} async-done(((bf16[16,128,256]{2,1,0:T(8,128)(2,1)}), bf16[16,128,256]{2,1,0:T(8,128)(2,1)S(1)}, u32[]{:S(2)}, u32[]{:S(2)}) %all-to-all-start) | async-done | bytes 1048608 | tf_op jit(solution)/shard_map/all_to_all | solution.py:58
  88.6 4.0 fusion.56
  92.5 97.4 %all-gather.6.cloned.1.call-done = bf16[1,512,4096]{2,1,0:T(8,128)(2,1)} async-done(((bf16[1,512,256]{2,1,0:T(8,128)(2,1)}), bf16[1,512,4096]{2,1,0:T(8,128)(2,1)}) %all-gather.6.cloned.1.call-update) | async-done | bytes 4194320 | tf_op jit(solution)/shard_map/all_gather | solution.py:66
  189.9 3.9 fusion.33
  193.8 2.7 fusion.41
  196.5 1.8 fusion.9
  198.2 10.2 %fusion.8 = bf16[2048,128]{1,0:T(8,128)(2,1)} fusion(bf16[128,4,128]{0,2,1:T(8,128)(2,1)S(1)} %bitcast.99, f32[128,4,2048]{2,0,1:T(8,128)} %fusion.41, f32[128,4,2048]{2,0,1:T(8,128)} %get-tuple-element.9, f32[128,4]{0,1:T(4,128)S(1)} %get-tuple-element.8), kind=kOutput, calls=%fused_computation.13 | convolution fusion | flops 276040192 | bytes 9046016 | tf_op jit(solution)/shard_map/tgj,tgh->jh/dot_general | solution.py:89
  208.5 9.2 %fusion.27 = bf16[128,4,128]{0,2,1:T(8,128)(2,1)} fusion(f32[128,4,2048]{2,0,1:T(8,128)} %fusion.41, bf16[2048,256]{1,0:T(8,128)(2,1)S(1)} %bitcast.93, f32[128,4,2048]{2,0,1:T(8,128)} %get-tuple-element.9, f32[128,4]{0,1:T(4,128)S(1)} %get-tuple-element.8), kind=kOutput, calls=%fused_computation.35 | convolution fusion | flops 275843584 | bytes 17436672 | tf_op jit(solution)/shard_map/tgj,jh->tgh/dot_general | solution.py:85
  217.7 195.6 %all-reduce.3.cloned.1.call-done = (bf16[2048,128]{1,0:T(8,128)(2,1)}, bf16[2048,128]{1,0:T(8,128)(2,1)}) async-done(((bf16[2048,128]{1,0:T(8,128)(2,1)}, bf16[2048,128]{1,0:T(8,128)(2,1)}), (bf16[2048,128]{1,0:T(8,128)(2,1)}, bf16[2048,128]{1,0:T(8,128)(2,1)})) %all-reduce.3.cloned.1.call-update) | async-done | bytes 1048592 | tf_op jit(solution)/shard_map/psum | solution.py:93
  413.4 2.0 copy.29
  415.4 2.0 copy.30
  417.5 102.9 %all-gather.4.cloned.1.call-done = bf16[2048,512]{0,1:T(8,128)(2,1)} async-done(((bf16[128,512]{0,1:T(8,128)(2,1)}), bf16[2048,512]{0,1:T(8,128)(2,1)}) %all-gather.4.cloned.1.call-update) | async-done | bytes 2097168 | tf_op jit(solution)/shard_map/all_gather | solution.py:98
  520.4 2.0 pad_maximum_fusion
  522.4 2.8 copy.31
  525.2 4.3 fusion.43
  529.5 10.1 %all-to-all-start.1 = ((f32[16,128,256]{2,1,0:T(8,128)}), f32[16,128,256]{2,1,0:T(8,128)S(1)}, u32[]{:S(2)}, u32[]{:S(2)}) async-start(f32[16,128,256]{2,1,0:T(8,128)} %fusion.43), calls=%async_computation.1 | async-start | bytes 4194304 | tf_op jit(solution)/shard_map/all_to_all | solution.py:102
  539.6 1.6 copy.19
  541.3 1.6 copy.33
  542.9 0.6 broadcast.84
  543.5 1.3 reduce.4
  544.8 1.3 mul.85
  546.1 0.6 fusion.19
  546.6 0.5 add_rsqrt_fusion
  547.2 73.2 %all-to-all-done.1 = f32[16,128,256]{2,1,0:T(8,128)S(1)} async-done(((f32[16,128,256]{2,1,0:T(8,128)}), f32[16,128,256]{2,1,0:T(8,128)S(1)}, u32[]{:S(2)}, u32[]{:S(2)}) %all-to-all-start.1) | async-done | bytes 2097184 | tf_op jit(solution)/shard_map/all_to_all | solution.py:102
  620.3 3.0 multiply_convert_fusion.1
  623.3 71.6 %all_to_all.37 = bf16[128,16,256]{2,0,1:T(8,128)(2,1)S(1)} all-to-all(bf16[128,16,256]{2,0,1:T(8,128)(2,1)S(1)} %get-tuple-element.6), channel_id=1, replica_groups=mesh['section'=32,'seq'=16] {'seq'}, dimensions={1} | all-to-all | bytes 2097152 | tf_op jit(solution)/shard_map/all_to_all | solution.py:63
  694.9 1.0 convolution_convert_fusion
  696.0 4.2 collective-permute-start.1
  700.2 1.5 collective-permute-done.1
  701.7 5.5 collective-permute-start.2
  707.2 2.3 copy.18
  709.5 1.9 copy.32
  711.3 0.7 broadcast_multiply_fusion
  712.0 4.7 collective-permute-done.2
  716.7 7.0 collective-permute-start.3
  723.7 2.3 fusion.18
  726.0 3.3 collective-permute-start
  729.3 2.8 collective-permute-done.3
  732.1 7.1 collective-permute-start.4
  739.2 10.9 %collective-permute-done.4 = bf16[256,768]{1,0:T(8,128)(2,1)S(1)} collective-permute-done((bf16[256,768]{1,0:T(8,128)(2,1)S(1)}, bf16[256,768]{1,0:T(8,128)(2,1)S(1)}, u32[]{:S(2)}, u32[]{:S(2)}) %collective-permute-start.4) | collective-permute-done | bytes 393248 | tf_op jit(solution)/shard_map/ppermute | solution.py:17
  750.1 6.9 collective-permute-start.5
  757.0 1.3 copy.34
  758.3 15.5 %collective-permute-done.5 = bf16[256,768]{1,0:T(8,128)(2,1)S(1)} collective-permute-done((bf16[256,768]{1,0:T(8,128)(2,1)S(1)}, bf16[256,768]{1,0:T(8,128)(2,1)S(1)}, u32[]{:S(2)}, u32[]{:S(2)}) %collective-permute-start.5) | collective-permute-done | bytes 393248 | tf_op jit(solution)/shard_map/ppermute | solution.py:17
  773.8 0.8 fusion.42
  (29 shorter events, 0.8 us)
Async XLA Ops:
  7.2 518.1 %copy-start = (bf16[1,256,768]{2,1,0:T(8,128)(2,1)S(1)}, bf16[1,256,768]{2,1,0:T(8,128)(2,1)}, u32[]{:S(2)}) copy-start(bf16[1,256,768]{2,1,0:T(8,128)(2,1)} %param.11) | copy-start | bytes 1179652
  7.2 20.5 %copy-start.7 = (s32[1,128]{1,0:T(1,128)S(1)}, s32[1,128]{1,0:T(1,128)}, u32[]{:S(2)}) copy-start(s32[1,128]{1,0:T(1,128)} %param.15) | copy-start | bytes 1540
  7.2 182.7 %all-gather.6.cloned.1.call-start = ((), (), s32[]{:S(2)}) async-start(), calls=%async_computation.4 | async-start | bytes 4456448 | tf_op jit(solution)/shard_map/all_gather | solution.py:66
  10.2 78.3 %all-to-all-start = ((bf16[16,128,256]{2,1,0:T(8,128)(2,1)}), bf16[16,128,256]{2,1,0:T(8,128)(2,1)S(1)}, u32[]{:S(2)}, u32[]{:S(2)}) async-start(bf16[16,128,256]{2,1,0:T(8,128)(2,1)} %stack.2), calls=%async_computation | async-start | bytes 2097152 | tf_op jit(solution)/shard_map/all_to_all | solution.py:58
  27.6 385.8 %all-reduce.3.cloned.1.call-start = ((), (), s32[]{:S(2)}) async-start(), calls=%async_computation.5 | async-start | bytes 2097152 | tf_op jit(solution)/shard_map/psum | solution.py:93
  88.6 101.3 %copy-start.1 = (bf16[1,128,4096]{2,1,0:T(8,128)(2,1)S(1)}, bf16[1,128,4096]{2,1,0:T(8,128)(2,1)}, u32[]{:S(2)}) copy-start(bf16[1,128,4096]{2,1,0:T(8,128)(2,1)} %param.10) | copy-start | bytes 3145732
  189.9 6.6 copy-start.8
  208.4 311.9 %all-gather.4.cloned.1.call-start = ((), (), s32[]{:S(2)}) async-start(), calls=%async_computation.3 | async-start | bytes 2228224 | tf_op jit(solution)/shard_map/all_gather | solution.py:98
  529.5 14.0 %copy-start.6 = (f32[1,4096]{1,0:T(1,128)S(1)}, f32[1,4096]{1,0:T(1,128)}, u32[]{:S(2)}) copy-start(f32[1,4096]{1,0:T(1,128)} %param.13) | copy-start | bytes 49156
  529.5 90.8 %all-to-all-start.1 = ((f32[16,128,256]{2,1,0:T(8,128)}), f32[16,128,256]{2,1,0:T(8,128)S(1)}, u32[]{:S(2)}, u32[]{:S(2)}) async-start(f32[16,128,256]{2,1,0:T(8,128)} %fusion.43), calls=%async_computation.1 | async-start | bytes 4194304 | tf_op jit(solution)/shard_map/all_to_all | solution.py:102
  620.3 74.6 %copy-start.2 = (bf16[2048,512]{0,1:T(8,128)(2,1)S(1)}, bf16[2048,512]{0,1:T(8,128)(2,1)}, u32[]{:S(2)}) copy-start(bf16[2048,512]{0,1:T(8,128)(2,1)} %all-gather.4.cloned.1.call-done) | copy-start | bytes 6291460
  620.3 74.6 %copy-start.3 = (bf16[2048,128]{0,1:T(8,128)(2,1)S(1)}, bf16[2048,128]{0,1:T(8,128)(2,1)}, u32[]{:S(2)}) copy-start(bf16[2048,128]{0,1:T(8,128)(2,1)} %copy.29) | copy-start | bytes 1572868
  620.3 74.6 %copy-start.4 = (bf16[2048,128]{0,1:T(8,128)(2,1)S(1)}, bf16[2048,128]{0,1:T(8,128)(2,1)}, u32[]{:S(2)}) copy-start(bf16[2048,128]{0,1:T(8,128)(2,1)} %copy.30) | copy-start | bytes 1572868
  696.0 5.7 collective-permute-start.1
  701.7 15.0 %collective-permute-start.2 = (bf16[256,768]{1,0:T(8,128)(2,1)}, bf16[256,768]{1,0:T(8,128)(2,1)}, u32[]{:S(2)}, u32[]{:S(2)}) collective-permute-start(bf16[256,768]{1,0:T(8,128)(2,1)} %collective-permute-done.1), channel_id=1, source_target_pairs={{0,32},{16,48},{32,0},{48,16},{64,96},{80,112},{96,64},{112,80},{1... | collective-permute-start | bytes 1179656 | tf_op jit(solution)/shard_map/ppermute | solution.py:17
  711.3 62.5 %copy-start.5 = (bf16[1,256,768]{2,1,0:T(8,128)(2,1)S(1)}, bf16[1,256,768]{2,1,0:T(8,128)(2,1)}, u32[]{:S(2)}) copy-start(bf16[1,256,768]{2,1,0:T(8,128)(2,1)} %param.14) | copy-start | bytes 1179652
  716.7 15.4 %collective-permute-start.3 = (bf16[256,768]{1,0:T(8,128)(2,1)}, bf16[256,768]{1,0:T(8,128)(2,1)S(1)}, u32[]{:S(2)}, u32[]{:S(2)}) collective-permute-start(bf16[256,768]{1,0:T(8,128)(2,1)} %collective-permute-done.2), channel_id=1, source_target_pairs={{0,64},{16,80},{32,96},{48,112},{64,0},{80,16},{96,32},{112,48},{1... | collective-permute-start | bytes 1179656 | tf_op jit(solution)/shard_map/ppermute | solution.py:17
  726.0 31.0 %collective-permute-start = (bf16[128,4096]{0,1:T(8,128)(2,1)S(1)}, bf16[128,4096]{0,1:T(8,128)(2,1)S(1)}, u32[]{:S(2)}, u32[]{:S(2)}) collective-permute-start(bf16[128,4096]{0,1:T(8,128)(2,1)S(1)} %fusion.18), channel_id=1, source_target_pairs={{0,16},{16,32},{32,48},{48,64},{64,80},{80,96},{96,112},{112,128},... | collective-permute-start | bytes 3145736 | tf_op jit(solution)/shard_map/ppermute | solution.py:13
  732.1 18.0 %collective-permute-start.4 = (bf16[256,768]{1,0:T(8,128)(2,1)S(1)}, bf16[256,768]{1,0:T(8,128)(2,1)S(1)}, u32[]{:S(2)}, u32[]{:S(2)}) collective-permute-start(bf16[256,768]{1,0:T(8,128)(2,1)S(1)} %collective-permute-done.3), channel_id=1, source_target_pairs={{0,128},{16,144},{32,160},{48,176},{64,192},{80,208},{96,224},{112... | collective-permute-start | bytes 1179656 | tf_op jit(solution)/shard_map/ppermute | solution.py:17
  750.1 23.7 %collective-permute-start.5 = (bf16[256,768]{1,0:T(8,128)(2,1)S(1)}, bf16[256,768]{1,0:T(8,128)(2,1)S(1)}, u32[]{:S(2)}, u32[]{:S(2)}) collective-permute-start(bf16[256,768]{1,0:T(8,128)(2,1)S(1)} %collective-permute-done.4), channel_id=1, source_target_pairs={{0,256},{16,272},{32,288},{48,304},{64,320},{80,336},{96,352},{112... | collective-permute-start | bytes 1179656 | tf_op jit(solution)/shard_map/ppermute | solution.py:17
Sparse Core Ops, SparseCore 0:
  11.0 178.8 all-gather.5
  208.6 204.7 all-reduce.2
  417.4 102.9 all-gather.3
